TPU v7x, 256 devices: a whole 4x4x8 slice. The times are simulated.
256 devices in a mesh: space: 32 (over z, x), section: 4 (over y), rep: 2 (over core).
Axes of the slice: x: 4, y: 4, z: 8, core: 2. Of those that a mesh axis runs over, the one named last changes fastest.
Arguments:
- feats: bfloat16 [4, 128, 40, 256], P('rep', 'space'), may hold values from -6 to 6
- labels: int32 [4, 128, 40], P('rep', 'space'), may hold values from 0 to 2
- class_weight: int32 [3], replicated, may hold values from 1 to 9
- depth_kernel: bfloat16 [4, 3, 9, 256], P('section'), may hold values from -2 to 2
- point_weight: bfloat16 [4, 4, 256, 256], P('section'), may hold values from -0.375 to 0.375
- proj_weight: bfloat16 [4, 1024, 256], P('section'), may hold values from -0.1875 to 0.1875
- head_weight: bfloat16 [4, 256, 3], P('section'), may hold values from -0.375 to 0.375
Outputs:
- kernel_grad: float32 [4, 3, 9, 256], P('section')
- point_grad: float32 [4, 4, 256, 256], P('section')
- proj_grad: float32 [4, 1024, 256], P('section')
- head_grad: float32 [4, 256, 3], P('section')
All inputs are finite; a program needn't handle non-finite values.
Results may differ from a plain program's by a relative error of at most 0.013.
The roundings to bfloat16 on the way count: a program that leaves them out, or rounds other values in their place, can miss the bound.
Values may be sent and summed in bfloat16 or wider, within the bound.
No kernel may reach another device: no remote copies, remote signals or barrier semaphores. Data moves between devices by JAX's collectives and lax.ppermute only.
A program may use at most 128 MiB of HBM per device.

v0:
```python
import jax
import jax.numpy as jnp
from jax import lax
from jax.sharding import PartitionSpec as P

spacings = (12, 24, 36)
loss_scale = 256.0


def recv_from(block, space_by, section_by):
    n_space = lax.axis_size("space")
    n_section = lax.axis_size("section")
    route = []
    for i in range(n_space):
        for s in range(n_section):
            si, ss = i + space_by, s + section_by
            if 0 <= si < n_space and 0 <= ss < n_section:
                route.append((si * n_section + ss, i * n_section + s))
    return lax.ppermute(block, ("space", "section"), route)


def moved(source, offset, axis_dim):
    length = source.shape[axis_dim]
    if abs(offset) >= length:
        return jnp.zeros_like(source)
    widths = [(0, 0)] * source.ndim
    widths[axis_dim] = (max(-offset, 0), max(offset, 0))
    padded = jnp.pad(source, widths)
    begin_at = max(offset, 0)
    return lax.slice_in_dim(padded, begin_at, begin_at + length, axis=axis_dim)


def matmul(first_op, second_op):
    return jnp.dot(first_op, second_op, preferred_element_type=jnp.float32)


def matmul_trans(first_op, second_op):
    return lax.dot_general(
        first_op, second_op, (((1,), (1,)), ((), ())), preferred_element_type=jnp.float32
    )


def outer(first_op, second_op):
    return lax.dot_general(
        first_op, second_op, (((0,), (0,)), ((), ())), preferred_element_type=jnp.float32
    )


def row_views_of(block, step):
    return [{a: moved(block, a * spacing // step, 2) for a in (-1, 1)} for spacing in spacings]


def forward_block(current, views, weights, label_tile, factor, weight_table, step):
    taps_all, point_mats, proj_mat, head_mat = weights
    snaps, tile_rows, width_cols, channels = current.shape
    pixels = snaps * tile_rows * width_cols
    plain_in = current.astype(jnp.float32)
    branch_maps = []
    for branch, spacing in enumerate(spacings):
        running = jnp.zeros(current.shape, jnp.float32)
        for row_tap in (-1, 0, 1):
            src = plain_in if row_tap == 0 else views[branch][row_tap].astype(jnp.float32)
            for col_tap in (-1, 0, 1):
                running = running + taps_all[branch, 3 * (row_tap + 1) + col_tap + 1] * moved(
                    src, col_tap * spacing // step, 1
                )
        branch_maps.append(running.astype(jnp.bfloat16))
    flat_in = current.reshape(pixels, channels)
    pre_acts = [matmul(branch_maps[b].reshape(pixels, channels), point_mats[b]) for b in range(3)]
    pre_acts.append(matmul(flat_in, point_mats[3]))
    joined = jnp.concatenate(
        [jnp.maximum(pre_act, 0.0).astype(jnp.bfloat16) for pre_act in pre_acts], axis=1
    )
    mixed_pre = matmul(joined, proj_mat)
    result = (flat_in.astype(jnp.float32) + jnp.maximum(mixed_pre, 0.0)).astype(jnp.bfloat16)
    logits = matmul(result, head_mat)
    class_ids = jnp.arange(3, dtype=jnp.int32)
    label_flat = label_tile.reshape(pixels, 1)
    onehot = (label_flat == class_ids[None, :]).astype(jnp.float32)
    pixel_weight = jnp.sum(onehot * weight_table[None, :], axis=1)
    chances = jax.nn.softmax(logits, axis=1)
    head_delta = ((factor * pixel_weight)[:, None] * (chances - onehot)).astype(jnp.bfloat16)
    head_term = outer(result, head_delta)
    from_head = matmul_trans(head_delta, head_mat)
    view_list = tuple(views[b][a] for b in range(3) for a in (-1, 1))
    record = (current, view_list, tuple(branch_maps), joined, mixed_pre, from_head)
    return result.reshape(current.shape), head_term, record


def backward_block(record, incoming, weights, step):
    taps_all, point_mats, proj_mat, head_mat = weights
    current, view_list, branch_maps, joined, mixed_pre, from_head = record
    snaps, tile_rows, width_cols, channels = current.shape
    pixels = snaps * tile_rows * width_cols
    total_grad = from_head + incoming
    gate_mixed = jnp.where(mixed_pre > 0, total_grad, 0.0).astype(jnp.bfloat16)
    proj_term = outer(joined, gate_mixed)
    back_joined = matmul_trans(gate_mixed, proj_mat)
    gate_joined = jnp.where(joined > 0, back_joined, 0.0).astype(jnp.bfloat16)
    flat_in = current.reshape(pixels, channels)
    point_terms = []
    branch_grads = []
    for branch in range(3):
        part_grad = gate_joined[:, branch * channels : (branch + 1) * channels]
        point_terms.append(outer(branch_maps[branch].reshape(pixels, channels), part_grad))
        branch_grads.append(
            matmul_trans(part_grad, point_mats[branch]).astype(jnp.bfloat16).reshape(current.shape)
        )
    part_grad = gate_joined[:, 3 * channels :]
    point_terms.append(outer(flat_in, part_grad))
    plain_back = matmul_trans(part_grad, point_mats[3])
    plain_in = current.astype(jnp.float32)
    local = jnp.zeros(current.shape, jnp.float32)
    kernel_terms = []
    for branch, spacing in enumerate(spacings):
        grad_wide = branch_grads[branch].astype(jnp.float32)
        rows = []
        for row_tap in (-1, 0, 1):
            if row_tap == 0:
                src = plain_in
            else:
                src = view_list[2 * branch + (0 if row_tap < 0 else 1)].astype(jnp.float32)
            for col_tap in (-1, 0, 1):
                partial_sum = jnp.sum(grad_wide * moved(src, col_tap * spacing // step, 1), axis=(0, 1))
                rows.append(jnp.sum(partial_sum, axis=0))
        for row_tap in (-1, 0, 1):
            row_moved = moved(grad_wide, -row_tap * spacing // step, 2)
            for col_tap in (-1, 0, 1):
                local = local + taps_all[branch, 3 * (row_tap + 1) + col_tap + 1] * moved(
                    row_moved, -col_tap * spacing // step, 1
                )
        kernel_terms.append(jnp.stack(rows))
    local = total_grad.reshape(current.shape) + plain_back.reshape(current.shape) + local
    return branch_grads, local, (jnp.stack(kernel_terms), jnp.stack(point_terms), proj_term)


def butterfly_sum(vec, axes, count):
    me = lax.axis_index(axes)
    buf = vec
    steps = count.bit_length() - 1
    for k in range(steps):
        bit = 1 << k
        half = buf.shape[0] // 2
        upper = (me // bit) % 2
        keep = lax.dynamic_slice_in_dim(buf, upper * half, half)
        send = lax.dynamic_slice_in_dim(buf, (1 - upper) * half, half)
        got = lax.ppermute(send, axes, [(i, i ^ bit) for i in range(count)])
        buf = keep + got
    for k in reversed(range(steps)):
        bit = 1 << k
        got = lax.ppermute(buf, axes, [(i, i ^ bit) for i in range(count)])
        upper = (me // bit) % 2 == 1
        buf = jnp.where(upper, jnp.concatenate([got, buf]), jnp.concatenate([buf, got]))
    return buf


def to_classes(block, step, space_count):
    snaps, rows, cols = block.shape[:3]
    rest = block.shape[3:]
    split = block.reshape((snaps, rows, cols // step, step) + rest)
    order = (0, 1, 3, 2) + tuple(range(4, split.ndim))
    send = split.transpose(order).reshape((space_count, cols // step) + rest)
    got = lax.all_to_all(send, "space", 0, 0, tiled=True)
    return jnp.swapaxes(got, 0, 1)[None]


def per_device(feats, labels, class_weight, depth_kernel, point_weight, proj_weight, head_weight):
    snaps, tile_rows, width_cols, channels = feats.shape
    space_count = lax.axis_size("space")
    section_count = lax.axis_size("section")
    rep_count = lax.axis_size("rep")
    section_place = lax.axis_index("section")
    factor = loss_scale / (snaps * rep_count * tile_rows * space_count * width_cols)
    weight_table = class_weight.astype(jnp.float32)
    taps_all = depth_kernel[0].astype(jnp.float32)
    weights = (taps_all, point_weight[0], proj_weight[0], head_weight[0])
    step = tile_rows
    assert snaps * tile_rows * step == space_count and width_cols % step == 0
    assert all(spacing % step == 0 for spacing in spacings)
    start_map = to_classes(feats, step, space_count)
    label_map = to_classes(labels, step, space_count)

    head_grad = jnp.zeros((channels, 3), jnp.float32)
    saved = None
    current = start_map
    for moment in range(section_count):
        is_valid = section_place == moment
        views = row_views_of(current, step)
        result, head_term, record = forward_block(
            current, views, weights, label_map, factor, weight_table, step
        )
        head_grad = jnp.where(is_valid, head_term, head_grad)
        if saved is None:
            saved = record
        else:
            saved = jax.tree.map(lambda new, old: jnp.where(is_valid, new, old), record, saved)
        if moment < section_count - 1:
            current = recv_from(result, 0, -1)

    kernel_grad = jnp.zeros((3, 9, channels), jnp.float32)
    point_grad = jnp.zeros((4, channels, channels), jnp.float32)
    proj_grad = jnp.zeros((4 * channels, channels), jnp.float32)
    pixels = start_map.size // channels
    incoming = jnp.zeros((pixels, channels), jnp.float32)
    for moment in range(section_count):
        is_valid = section_place == section_count - 1 - moment
        branch_grads, local, terms = backward_block(saved, incoming, weights, step)
        kernel_grad = jnp.where(is_valid, terms[0], kernel_grad)
        point_grad = jnp.where(is_valid, terms[1], point_grad)
        proj_grad = jnp.where(is_valid, terms[2], proj_grad)
        if moment < section_count - 1:
            arriving = recv_from(local.astype(jnp.bfloat16), 0, 1)
            incoming = arriving.astype(jnp.float32).reshape(pixels, channels)

    parts = (kernel_grad, point_grad, proj_grad, head_grad)
    flat = jnp.concatenate([p.reshape(-1) for p in parts])
    group = space_count * rep_count
    chunk = group * 128
    padded = (flat.shape[0] + chunk - 1) // chunk * chunk
    flat = jnp.pad(flat, (0, padded - flat.shape[0]))
    total = butterfly_sum(flat, ("space", "rep"), group)
    outs = []
    start = 0
    for p in parts:
        outs.append(total[start : start + p.size].reshape((1,) + p.shape))
        start += p.size
    return tuple(outs)


def solution(mesh):
    placed = (
        P("rep", "space", None, None),
        P("rep", "space", None),
        P(),
        P("section", None, None, None),
        P("section", None, None, None),
        P("section", None, None),
        P("section", None, None),
    )
    return jax.shard_map(
        per_device,
        mesh=mesh,
        in_specs=placed,
        out_specs=(
            P("section", None, None, None),
            P("section", None, None, None),
            P("section", None, None),
            P("section", None, None),
        ),
        check_vma=False,
    )
```

profile of v0, /device:TPU:25, one launch (start us, length us, event | category | flops | bytes accessed | tf_op | source)
XLA Modules:
  0.0 240.8 jit_solution(15467920879587703649)
XLA Ops:
  2.2 11.0 %all-to-all-start.1 = ((s32[32,1,10]{2,1,0:T(1,128)}), s32[32,1,10]{2,1,0:T(1,128)S(1)}, u32[]{:S(2)}, u32[]{:S(2)}) async-start(s32[32,1,10]{2,1,0:T(1,128)} %bitcast.65), calls=%async_computation.1 | async-start | bytes 32768 | tf_op jit(solution)/shard_map/all_to_all | solution.py:163
  14.3 1.0 reshape.547
  16.6 5.2 %all-to-all-done.1 = s32[32,1,10]{2,1,0:T(1,128)S(1)} async-done(((s32[32,1,10]{2,1,0:T(1,128)}), s32[32,1,10]{2,1,0:T(1,128)S(1)}, u32[]{:S(2)}, u32[]{:S(2)}) %all-to-all-start.1) | async-done | bytes 1312 | tf_op jit(solution)/shard_map/all_to_all | solution.py:163
  21.8 4.1 %all-to-all-start = ((bf16[32,10,256]{2,1,0:T(8,128)(2,1)}), bf16[32,10,256]{2,1,0:T(8,128)(2,1)S(1)}, u32[]{:S(2)}, u32[]{:S(2)}) async-start(bf16[32,10,256]{2,1,0:T(8,128)(2,1)} %bitcast.3), calls=%async_computation | async-start | bytes 524288 | tf_op jit(solution)/shard_map/all_to_all | solution.py:163
  26.1 10.1 %all-to-all-done = bf16[32,10,256]{2,1,0:T(8,128)(2,1)S(1)} async-done(((bf16[32,10,256]{2,1,0:T(8,128)(2,1)}), bf16[32,10,256]{2,1,0:T(8,128)(2,1)S(1)}, u32[]{:S(2)}, u32[]{:S(2)}) %all-to-all-start) | async-done | bytes 163872 | tf_op jit(solution)/shard_map/all_to_all | solution.py:163
  38.9 1.3 collective-permute-start
  40.5 4.6 %collective-permute-done = bf16[1,10,32,256]{3,2,1,0:T(8,128)(2,1)S(1)} collective-permute-done((bf16[1,10,32,256]{3,2,1,0:T(8,128)(2,1)S(1)}, bf16[1,10,32,256]{3,2,1,0:T(8,128)(2,1)S(1)}, u32[]{:S(2)}, u32[]{:S(2)}) %collective-permute-start) | collective-permute-done | bytes 163872 | tf_op jit(solution)/shard_map/ppermute | solution.py:19
  47.0 1.3 collective-permute-start.1
  48.5 4.5 %collective-permute-done.1 = bf16[1,10,32,256]{3,2,1,0:T(8,128)(2,1)S(1)} collective-permute-done((bf16[1,10,32,256]{3,2,1,0:T(8,128)(2,1)S(1)}, bf16[1,10,32,256]{3,2,1,0:T(8,128)(2,1)S(1)}, u32[]{:S(2)}, u32[]{:S(2)}) %collective-permute-start.1) | collective-permute-done | bytes 163872 | tf_op jit(solution)/shard_map/ppermute | solution.py:19
  55.0 1.3 collective-permute-start.2
  56.5 4.6 %collective-permute-done.2 = bf16[1,10,32,256]{3,2,1,0:T(8,128)(2,1)S(1)} collective-permute-done((bf16[1,10,32,256]{3,2,1,0:T(8,128)(2,1)S(1)}, bf16[1,10,32,256]{3,2,1,0:T(8,128)(2,1)S(1)}, u32[]{:S(2)}, u32[]{:S(2)}) %collective-permute-start.2) | collective-permute-done | bytes 163872 | tf_op jit(solution)/shard_map/ppermute | solution.py:19
  61.1 1.1 fusion.609
  68.7 1.7 fusion.7
  70.3 3.0 %collective-permute-start.3 = (bf16[1,10,32,256]{3,2,1,0:T(8,128)(2,1)}, bf16[1,10,32,256]{3,2,1,0:T(8,128)(2,1)}, u32[]{:S(2)}, u32[]{:S(2)}) collective-permute-start(bf16[1,10,32,256]{3,2,1,0:T(8,128)(2,1)} %fusion.7), channel_id=1, source_target_pairs={{2,0},{4,2},{6,4},{10,8},{12,10},{14,12},{18,16},{20,18},{22,20},{... | collective-permute-start | bytes 491528 | tf_op jit(solution)/shard_map/ppermute | solution.py:19
  73.9 1.5 convolution_select_fusion.4
  77.6 1.5 copy.22
  79.0 1.7 reshape.582
  83.9 1.0 convolution_bitcast_fusion.7
  87.2 1.8 collective-permute-start.4
  89.5 1.0 convolution_bitcast_fusion.6
  90.4 1.0 convolution_bitcast_fusion.5
  93.7 1.0 convolution_bitcast_fusion
  94.7 1.0 convolution_bitcast_fusion.4
  95.6 1.0 convolution_bitcast_fusion.11
  96.6 1.0 convolution_bitcast_fusion.10
  99.6 3.9 %collective-permute-start.5 = (bf16[1,10,32,256]{3,2,1,0:T(8,128)(2,1)S(1)}, bf16[1,10,32,256]{3,2,1,0:T(8,128)(2,1)S(1)}, u32[]{:S(2)}, u32[]{:S(2)}) collective-permute-start(bf16[1,10,32,256]{3,2,1,0:T(8,128)(2,1)S(1)} %fusion.353), channel_id=1, source_target_pairs={{2,0},{4,2},{6,4},{10,8},{12,10},{14,12},{18,16},{20,18},{22,20},{... | collective-permute-start | bytes 491528 | tf_op jit(solution)/shard_map/ppermute | solution.py:19
  103.6 1.5 convolution_select_fusion.6
  105.0 1.3 fusion.359
  106.3 1.0 convolution_bitcast_fusion.9
  109.4 1.0 convolution_bitcast_fusion.15
  110.4 1.0 convolution_bitcast_fusion.14
  111.4 1.0 convolution_bitcast_fusion.13
  112.4 1.0 convolution_bitcast_fusion.12
  113.3 1.1 fusion.357
  114.8 1.2 fusion.361
  116.2 1.0 fusion.365
  117.5 1.0 fusion.373
  118.5 1.4 stack.590
  120.7 1.4 stack.556
  122.2 1.3 stack.522
  124.5 2.0 maximum_select_fusion.2
  129.1 1.1 dynamic_slice.37
  130.2 8.9 %collective-permute-start.6 = (f32[266240]{0:T(1024)}, f32[266240]{0:T(1024)}, u32[]{:S(2)}, u32[]{:S(2)}) collective-permute-start(f32[266240]{0:T(1024)} %dynamic_slice.37), channel_id=1, source_target_pairs={{0,1},{1,0},{8,9},{9,8},{16,17},{17,16},{24,25},{25,24},{32,33},{3... | collective-permute-start | bytes 3194888 | tf_op jit(solution)/shard_map/ppermute | solution.py:147
  139.1 2.7 %collective-permute-done.6 = f32[266240]{0:T(1024)} collective-permute-done((f32[266240]{0:T(1024)}, f32[266240]{0:T(1024)}, u32[]{:S(2)}, u32[]{:S(2)}) %collective-permute-start.6) | collective-permute-done | bytes 1064992 | tf_op jit(solution)/shard_map/ppermute | solution.py:147
  141.7 1.3 dynamic-slice_add_fusion
  143.1 1.0 copy-done.13
  144.3 13.2 %collective-permute-done.7 = f32[133120]{0:T(1024)S(1)} collective-permute-done((f32[133120]{0:T(1024)S(1)}, f32[133120]{0:T(1024)S(1)}, u32[]{:S(2)}, u32[]{:S(2)}) %collective-permute-start.7) | collective-permute-done | bytes 532512 | tf_op jit(solution)/shard_map/ppermute | solution.py:147
  157.5 1.1 dynamic-slice_add_fusion.1
  158.6 1.1 collective-permute-start.8
  159.7 7.2 %collective-permute-done.8 = f32[66560]{0:T(1024)S(1)} collective-permute-done((f32[66560]{0:T(1024)S(1)}, f32[66560]{0:T(1024)S(1)}, u32[]{:S(2)}, u32[]{:S(2)}) %collective-permute-start.8) | collective-permute-done | bytes 266272 | tf_op jit(solution)/shard_map/ppermute | solution.py:147
  167.6 3.5 %collective-permute-done.9 = f32[33280]{0:T(1024)S(1)} collective-permute-done((f32[33280]{0:T(1024)S(1)}, f32[33280]{0:T(1024)S(1)}, u32[]{:S(2)}, u32[]{:S(2)}) %collective-permute-start.9) | collective-permute-done | bytes 133152 | tf_op jit(solution)/shard_map/ppermute | solution.py:147
  171.9 4.2 %collective-permute-done.10 = f32[16640]{0:T(1024)S(1)} collective-permute-done((f32[16640]{0:T(1024)S(1)}, f32[16640]{0:T(1024)S(1)}, u32[]{:S(2)}, u32[]{:S(2)}) %collective-permute-start.10) | collective-permute-done | bytes 66592 | tf_op jit(solution)/shard_map/ppermute | solution.py:147
  176.7 6.8 %collective-permute-done.11 = f32[8320]{0:T(1024)S(1)} collective-permute-done((f32[8320]{0:T(1024)S(1)}, f32[8320]{0:T(1024)S(1)}, u32[]{:S(2)}, u32[]{:S(2)}) %collective-permute-start.11) | collective-permute-done | bytes 33312 | tf_op jit(solution)/shard_map/ppermute | solution.py:147
  183.6 7.1 %collective-permute-done.12 = f32[8320]{0:T(1024)S(1)} collective-permute-done((f32[8320]{0:T(1024)S(1)}, f32[8320]{0:T(1024)S(1)}, u32[]{:S(2)}, u32[]{:S(2)}) %collective-permute-start.12) | collective-permute-done | bytes 33312 | tf_op jit(solution)/shard_map/ppermute | solution.py:151
  190.9 4.9 %collective-permute-done.13 = f32[16640]{0:T(1024)S(1)} collective-permute-done((f32[16640]{0:T(1024)S(1)}, f32[16640]{0:T(1024)S(1)}, u32[]{:S(2)}, u32[]{:S(2)}) %collective-permute-start.13) | collective-permute-done | bytes 66592 | tf_op jit(solution)/shard_map/ppermute | solution.py:151
  195.8 3.8 %collective-permute-done.14 = f32[33280]{0:T(1024)S(1)} collective-permute-done((f32[33280]{0:T(1024)S(1)}, f32[33280]{0:T(1024)S(1)}, u32[]{:S(2)}, u32[]{:S(2)}) %collective-permute-start.14) | collective-permute-done | bytes 133152 | tf_op jit(solution)/shard_map/ppermute | solution.py:151
  200.5 6.1 %collective-permute-done.15 = f32[66560]{0:T(1024)S(1)} collective-permute-done((f32[66560]{0:T(1024)S(1)}, f32[66560]{0:T(1024)S(1)}, u32[]{:S(2)}, u32[]{:S(2)}) %collective-permute-start.15) | collective-permute-done | bytes 266272 | tf_op jit(solution)/shard_map/ppermute | solution.py:151
  206.7 11.2 %collective-permute-done.16 = f32[133120]{0:T(1024)S(1)} collective-permute-done((f32[133120]{0:T(1024)S(1)}, f32[133120]{0:T(1024)S(1)}, u32[]{:S(2)}, u32[]{:S(2)}) %collective-permute-start.16) | collective-permute-done | bytes 532512 | tf_op jit(solution)/shard_map/ppermute | solution.py:151
  218.1 10.4 %collective-permute-start.17 = (f32[266240]{0:T(1024)S(1)}, f32[266240]{0:T(1024)}, u32[]{:S(2)}, u32[]{:S(2)}) collective-permute-start(f32[266240]{0:T(1024)S(1)} %maximum_select_fusion.1), channel_id=1, source_target_pairs={{0,1},{1,0},{8,9},{9,8},{16,17},{17,16},{24,25},{25,24},{32,33},{3... | collective-permute-start | bytes 3194888 | tf_op jit(solution)/shard_map/ppermute | solution.py:151
  228.5 2.4 %collective-permute-done.17 = f32[266240]{0:T(1024)} collective-permute-done((f32[266240]{0:T(1024)S(1)}, f32[266240]{0:T(1024)}, u32[]{:S(2)}, u32[]{:S(2)}) %collective-permute-start.17) | collective-permute-done | bytes 1064992 | tf_op jit(solution)/shard_map/ppermute | solution.py:151
  231.0 2.5 %maximum_select_fusion = f32[532480]{0:T(1024)S(1)} fusion(f32[266240]{0:T(1024)} %copy-done.12, f32[266240]{0:T(1024)} %collective-permute-done.17, pred[]{:T(512)S(6)} %eq.41), kind=kLoop, calls=%fused_computation.4 | loop fusion | flops 1597440 | bytes 4259841 | tf_op jit(solution)/shard_map/jit(_where)/select_n | solution.py:153
  233.5 1.6 fusion.616
  235.4 2.6 %reshape.584 = f32[1,4,256,256]{3,2,1,0:T(8,128)} reshape(f32[262144]{0:T(1024)} %get-tuple-element.223) | data formatting | bytes 2097152 | tf_op jit(solution)/shard_map/reshape | solution.py:225
  238.0 1.3 reshape.585
  (439 shorter events, 41.8 us)
Async XLA Ops:
  0.6 37.9 %copy-start = (bf16[1,1024,256]{2,1,0:T(8,128)(2,1)S(1)}, bf16[1,1024,256]{2,1,0:T(8,128)(2,1)}, u32[]{:S(2)}) copy-start(bf16[1,1024,256]{2,1,0:T(8,128)(2,1)} %param.12) | copy-start | bytes 1572868
  2.2 19.6 %all-to-all-start.1 = ((s32[32,1,10]{2,1,0:T(1,128)}), s32[32,1,10]{2,1,0:T(1,128)S(1)}, u32[]{:S(2)}, u32[]{:S(2)}) async-start(s32[32,1,10]{2,1,0:T(1,128)} %bitcast.65), calls=%async_computation.1 | async-start | bytes 32768 | tf_op jit(solution)/shard_map/all_to_all | solution.py:163
  14.0 48.7 %copy-start.54 = (f32[1,1,256]{2,0,1:T(1,128)}, f32[1,1,256]{2,0,1:T(1,128)S(1)}, u32[]{:S(2)}) copy-start(f32[1,1,256]{2,0,1:T(1,128)S(1)} %get-tuple-element.287) | copy-start | bytes 3076
  14.0 48.7 %copy-start.57 = (f32[1,1,256]{2,0,1:T(1,128)}, f32[1,1,256]{2,0,1:T(1,128)S(1)}, u32[]{:S(2)}) copy-start(f32[1,1,256]{2,0,1:T(1,128)S(1)} %get-tuple-element.288) | copy-start | bytes 3076
  14.0 48.7 %copy-start.60 = (f32[1,1,256]{2,0,1:T(1,128)}, f32[1,1,256]{2,0,1:T(1,128)S(1)}, u32[]{:S(2)}) copy-start(f32[1,1,256]{2,0,1:T(1,128)S(1)} %get-tuple-element.289) | copy-start | bytes 3076
  14.0 48.7 %copy-start.63 = (f32[1,1,256]{2,0,1:T(1,128)}, f32[1,1,256]{2,0,1:T(1,128)S(1)}, u32[]{:S(2)}) copy-start(f32[1,1,256]{2,0,1:T(1,128)S(1)} %get-tuple-element.290) | copy-start | bytes 3076
  14.0 48.7 %copy-start.66 = (f32[1,1,256]{2,0,1:T(1,128)}, f32[1,1,256]{2,0,1:T(1,128)S(1)}, u32[]{:S(2)}) copy-start(f32[1,1,256]{2,0,1:T(1,128)S(1)} %get-tuple-element.291) | copy-start | bytes 3076
  14.1 48.7 %copy-start.69 = (f32[1,1,256]{2,0,1:T(1,128)}, f32[1,1,256]{2,0,1:T(1,128)S(1)}, u32[]{:S(2)}) copy-start(f32[1,1,256]{2,0,1:T(1,128)S(1)} %get-tuple-element.292) | copy-start | bytes 3076
  14.1 48.7 %copy-start.72 = (f32[1,1,256]{2,0,1:T(1,128)}, f32[1,1,256]{2,0,1:T(1,128)S(1)}, u32[]{:S(2)}) copy-start(f32[1,1,256]{2,0,1:T(1,128)S(1)} %get-tuple-element.293) | copy-start | bytes 3076
  14.1 53.9 %copy-start.38 = (f32[1,1,256]{2,0,1:T(1,128)}, f32[1,1,256]{2,0,1:T(1,128)S(1)}, u32[]{:S(2)}) copy-start(f32[1,1,256]{2,0,1:T(1,128)S(1)} %get-tuple-element.279) | copy-start | bytes 3076
  14.1 53.9 %copy-start.40 = (f32[1,1,256]{2,0,1:T(1,128)}, f32[1,1,256]{2,0,1:T(1,128)S(1)}, u32[]{:S(2)}) copy-start(f32[1,1,256]{2,0,1:T(1,128)S(1)} %get-tuple-element.280) | copy-start | bytes 3076
  14.1 53.9 %copy-start.42 = (f32[1,1,256]{2,0,1:T(1,128)}, f32[1,1,256]{2,0,1:T(1,128)S(1)}, u32[]{:S(2)}) copy-start(f32[1,1,256]{2,0,1:T(1,128)S(1)} %get-tuple-element.281) | copy-start | bytes 3076
  14.1 53.9 %copy-start.44 = (f32[1,1,256]{2,0,1:T(1,128)}, f32[1,1,256]{2,0,1:T(1,128)S(1)}, u32[]{:S(2)}) copy-start(f32[1,1,256]{2,0,1:T(1,128)S(1)} %get-tuple-element.282) | copy-start | bytes 3076
  14.1 53.9 %copy-start.46 = (f32[1,1,256]{2,0,1:T(1,128)}, f32[1,1,256]{2,0,1:T(1,128)S(1)}, u32[]{:S(2)}) copy-start(f32[1,1,256]{2,0,1:T(1,128)S(1)} %get-tuple-element.283) | copy-start | bytes 3076
  14.1 53.9 %copy-start.48 = (f32[1,1,256]{2,0,1:T(1,128)}, f32[1,1,256]{2,0,1:T(1,128)S(1)}, u32[]{:S(2)}) copy-start(f32[1,1,256]{2,0,1:T(1,128)S(1)} %get-tuple-element.284) | copy-start | bytes 3076
  14.1 53.9 %copy-start.50 = (f32[1,1,256]{2,0,1:T(1,128)}, f32[1,1,256]{2,0,1:T(1,128)S(1)}, u32[]{:S(2)}) copy-start(f32[1,1,256]{2,0,1:T(1,128)S(1)} %get-tuple-element.285) | copy-start | bytes 3076
  14.1 53.9 %copy-start.52 = (f32[1,1,256]{2,0,1:T(1,128)}, f32[1,1,256]{2,0,1:T(1,128)S(1)}, u32[]{:S(2)}) copy-start(f32[1,1,256]{2,0,1:T(1,128)S(1)} %get-tuple-element.286) | copy-start | bytes 3076
  14.2 48.0 %copy-start.75 = (f32[1,1,256]{2,0,1:T(1,128)}, f32[1,1,256]{2,0,1:T(1,128)S(1)}, u32[]{:S(2)}) copy-start(f32[1,1,256]{2,0,1:T(1,128)S(1)} %get-tuple-element.294) | copy-start | bytes 3076
  14.2 48.0 %copy-start.78 = (f32[1,1,256]{2,0,1:T(1,128)}, f32[1,1,256]{2,0,1:T(1,128)S(1)}, u32[]{:S(2)}) copy-start(f32[1,1,256]{2,0,1:T(1,128)S(1)} %get-tuple-element.295) | copy-start | bytes 3076
  14.2 48.0 %copy-start.81 = (f32[1,1,256]{2,0,1:T(1,128)}, f32[1,1,256]{2,0,1:T(1,128)S(1)}, u32[]{:S(2)}) copy-start(f32[1,1,256]{2,0,1:T(1,128)S(1)} %get-tuple-element.296) | copy-start | bytes 3076
  14.2 48.0 %copy-start.84 = (f32[1,1,256]{2,0,1:T(1,128)}, f32[1,1,256]{2,0,1:T(1,128)S(1)}, u32[]{:S(2)}) copy-start(f32[1,1,256]{2,0,1:T(1,128)S(1)} %get-tuple-element.297) | copy-start | bytes 3076
  14.2 48.0 %copy-start.87 = (f32[1,1,256]{2,0,1:T(1,128)}, f32[1,1,256]{2,0,1:T(1,128)S(1)}, u32[]{:S(2)}) copy-start(f32[1,1,256]{2,0,1:T(1,128)S(1)} %get-tuple-element.298) | copy-start | bytes 3076
  14.2 48.0 %copy-start.90 = (f32[1,1,256]{2,0,1:T(1,128)}, f32[1,1,256]{2,0,1:T(1,128)S(1)}, u32[]{:S(2)}) copy-start(f32[1,1,256]{2,0,1:T(1,128)S(1)} %get-tuple-element.299) | copy-start | bytes 3076
  14.2 48.0 %copy-start.93 = (f32[1,1,256]{2,0,1:T(1,128)}, f32[1,1,256]{2,0,1:T(1,128)S(1)}, u32[]{:S(2)}) copy-start(f32[1,1,256]{2,0,1:T(1,128)S(1)} %get-tuple-element.300) | copy-start | bytes 3076
  14.2 48.0 %copy-start.96 = (f32[1,1,256]{2,0,1:T(1,128)}, f32[1,1,256]{2,0,1:T(1,128)S(1)}, u32[]{:S(2)}) copy-start(f32[1,1,256]{2,0,1:T(1,128)S(1)} %get-tuple-element.301) | copy-start | bytes 3076
  21.8 14.5 %all-to-all-start = ((bf16[32,10,256]{2,1,0:T(8,128)(2,1)}), bf16[32,10,256]{2,1,0:T(8,128)(2,1)S(1)}, u32[]{:S(2)}, u32[]{:S(2)}) async-start(bf16[32,10,256]{2,1,0:T(8,128)(2,1)} %bitcast.3), calls=%async_computation | async-start | bytes 524288 | tf_op jit(solution)/shard_map/all_to_all | solution.py:163
  38.9 6.1 %collective-permute-start = (bf16[1,10,32,256]{3,2,1,0:T(8,128)(2,1)S(1)}, bf16[1,10,32,256]{3,2,1,0:T(8,128)(2,1)S(1)}, u32[]{:S(2)}, u32[]{:S(2)}) collective-permute-start(bf16[1,10,32,256]{3,2,1,0:T(8,128)(2,1)S(1)} %bitcast.583), channel_id=1, source_target_pairs={{0,2},{2,4},{4,6},{8,10},{10,12},{12,14},{16,18},{18,20},{20,22},{... | collective-permute-start | bytes 491528 | tf_op jit(solution)/shard_map/ppermute | solution.py:19
  47.0 6.1 %collective-permute-start.1 = (bf16[1,10,32,256]{3,2,1,0:T(8,128)(2,1)S(1)}, bf16[1,10,32,256]{3,2,1,0:T(8,128)(2,1)S(1)}, u32[]{:S(2)}, u32[]{:S(2)}) collective-permute-start(bf16[1,10,32,256]{3,2,1,0:T(8,128)(2,1)S(1)} %bitcast.584), channel_id=1, source_target_pairs={{0,2},{2,4},{4,6},{8,10},{10,12},{12,14},{16,18},{18,20},{20,22},{... | collective-permute-start | bytes 491528 | tf_op jit(solution)/shard_map/ppermute | solution.py:19
  55.0 6.1 %collective-permute-start.2 = (bf16[1,10,32,256]{3,2,1,0:T(8,128)(2,1)S(1)}, bf16[1,10,32,256]{3,2,1,0:T(8,128)(2,1)S(1)}, u32[]{:S(2)}, u32[]{:S(2)}) collective-permute-start(bf16[1,10,32,256]{3,2,1,0:T(8,128)(2,1)S(1)} %bitcast.585), channel_id=1, source_target_pairs={{0,2},{2,4},{4,6},{8,10},{10,12},{12,14},{16,18},{18,20},{20,22},{... | collective-permute-start | bytes 491528 | tf_op jit(solution)/shard_map/ppermute | solution.py:19
  62.5 10.8 %copy-start.17 = (bf16[1,10,32,256]{3,2,1,0:T(8,128)(2,1)}, bf16[1,10,32,256]{3,2,1,0:T(8,128)(2,1)S(1)}, u32[]{:S(2)}) copy-start(bf16[1,10,32,256]{3,2,1,0:T(8,128)(2,1)S(1)} %get-tuple-element.212) | copy-start | bytes 491524
  63.1 10.5 %copy-start.19 = (bf16[1,10,32,256]{3,2,1,0:T(8,128)(2,1)}, bf16[1,10,32,256]{3,2,1,0:T(8,128)(2,1)S(1)}, u32[]{:S(2)}) copy-start(bf16[1,10,32,256]{3,2,1,0:T(8,128)(2,1)S(1)} %get-tuple-element.214) | copy-start | bytes 491524
  63.6 13.0 %copy-start.21 = (bf16[1,10,32,256]{3,2,1,0:T(8,128)(2,1)}, bf16[1,10,32,256]{3,2,1,0:T(8,128)(2,1)S(1)}, u32[]{:S(2)}) copy-start(bf16[1,10,32,256]{3,2,1,0:T(8,128)(2,1)S(1)} %get-tuple-element.216) | copy-start | bytes 491524
  66.4 7.6 %copy-start.10 = (pred[320,256]{1,0:T(32,128)(4,1)}, pred[320,256]{1,0:T(32,128)(4,1)S(1)}, u32[]{:S(2)}) copy-start(pred[320,256]{1,0:T(32,128)(4,1)S(1)} %select_compare_fusion) | copy-start | bytes 245764
  70.3 11.1 %collective-permute-start.3 = (bf16[1,10,32,256]{3,2,1,0:T(8,128)(2,1)}, bf16[1,10,32,256]{3,2,1,0:T(8,128)(2,1)}, u32[]{:S(2)}, u32[]{:S(2)}) collective-permute-start(bf16[1,10,32,256]{3,2,1,0:T(8,128)(2,1)} %fusion.7), channel_id=1, source_target_pairs={{2,0},{4,2},{6,4},{10,8},{12,10},{14,12},{18,16},{20,18},{22,20},{... | collective-permute-start | bytes 491528 | tf_op jit(solution)/shard_map/ppermute | solution.py:19
  73.9 6.8 %copy-start.28 = (bf16[1,10,32,256]{3,2,1,0:T(8,128)(2,1)S(1)}, bf16[1,10,32,256]{3,2,1,0:T(8,128)(2,1)}, u32[]{:S(2)}) copy-start(bf16[1,10,32,256]{3,2,1,0:T(8,128)(2,1)} %copy-done.27) | copy-start | bytes 491524
  87.2 4.3 %collective-permute-start.4 = (bf16[1,10,32,256]{3,2,1,0:T(8,128)(2,1)S(1)}, bf16[1,10,32,256]{3,2,1,0:T(8,128)(2,1)S(1)}, u32[]{:S(2)}, u32[]{:S(2)}) collective-permute-start(bf16[1,10,32,256]{3,2,1,0:T(8,128)(2,1)S(1)} %fusion.342), channel_id=1, source_target_pairs={{2,0},{4,2},{6,4},{10,8},{12,10},{14,12},{18,16},{20,18},{22,20},{... | collective-permute-start | bytes 491528 | tf_op jit(solution)/shard_map/ppermute | solution.py:19
  99.6 8.6 %collective-permute-start.5 = (bf16[1,10,32,256]{3,2,1,0:T(8,128)(2,1)S(1)}, bf16[1,10,32,256]{3,2,1,0:T(8,128)(2,1)S(1)}, u32[]{:S(2)}, u32[]{:S(2)}) collective-permute-start(bf16[1,10,32,256]{3,2,1,0:T(8,128)(2,1)S(1)} %fusion.353), channel_id=1, source_target_pairs={{2,0},{4,2},{6,4},{10,8},{12,10},{14,12},{18,16},{20,18},{22,20},{... | collective-permute-start | bytes 491528 | tf_op jit(solution)/shard_map/ppermute | solution.py:19
  117.3 6.3 %copy-start.117 = (f32[256]{0:T(256)S(1)}, f32[256]{0:T(256)}, u32[]{:S(2)}) copy-start(f32[256]{0:T(256)} %get-tuple-element.177) | copy-start | bytes 3076
  117.3 6.3 %copy-start.118 = (f32[256]{0:T(256)S(1)}, f32[256]{0:T(256)}, u32[]{:S(2)}) copy-start(f32[256]{0:T(256)} %get-tuple-element.178) | copy-start | bytes 3076
  117.3 6.3 %copy-start.119 = (f32[256]{0:T(256)S(1)}, f32[256]{0:T(256)}, u32[]{:S(2)}) copy-start(f32[256]{0:T(256)} %get-tuple-element.179) | copy-start | bytes 3076
  117.3 6.3 %copy-start.122 = (f32[256]{0:T(256)S(1)}, f32[256]{0:T(256)}, u32[]{:S(2)}) copy-start(f32[256]{0:T(256)} %get-tuple-element.102) | copy-start | bytes 3076
  117.3 6.3 %copy-start.113 = (f32[256]{0:T(256)S(1)}, f32[256]{0:T(256)}, u32[]{:S(2)}) copy-start(f32[256]{0:T(256)} %get-tuple-element.180) | copy-start | bytes 3076
  117.4 6.3 %copy-start.114 = (f32[256]{0:T(256)S(1)}, f32[256]{0:T(256)}, u32[]{:S(2)}) copy-start(f32[256]{0:T(256)} %get-tuple-element.181) | copy-start | bytes 3076
  117.4 6.3 %copy-start.115 = (f32[256]{0:T(256)S(1)}, f32[256]{0:T(256)}, u32[]{:S(2)}) copy-start(f32[256]{0:T(256)} %get-tuple-element.184) | copy-start | bytes 3076
  117.4 6.3 %copy-start.116 = (f32[256]{0:T(256)S(1)}, f32[256]{0:T(256)}, u32[]{:S(2)}) copy-start(f32[256]{0:T(256)} %get-tuple-element.185) | copy-start | bytes 3076
  117.4 6.3 %copy-start.132 = (f32[256]{0:T(256)S(1)}, f32[256]{0:T(256)}, u32[]{:S(2)}) copy-start(f32[256]{0:T(256)} %get-tuple-element.130) | copy-start | bytes 3076
  117.4 6.3 %copy-start.133 = (f32[256]{0:T(256)S(1)}, f32[256]{0:T(256)}, u32[]{:S(2)}) copy-start(f32[256]{0:T(256)} %get-tuple-element.131) | copy-start | bytes 3076
  117.4 6.3 %copy-start.134 = (f32[256]{0:T(256)S(1)}, f32[256]{0:T(256)}, u32[]{:S(2)}) copy-start(f32[256]{0:T(256)} %get-tuple-element.162) | copy-start | bytes 3076
  117.4 7.0 %copy-start.32 = (f32[1,256,256]{2,1,0:T(8,128)S(1)}, f32[1,256,256]{2,1,0:T(8,128)}, u32[]{:S(2)}) copy-start(f32[1,256,256]{2,1,0:T(8,128)} %convolution_bitcast_fusion.1) | copy-start | bytes 786436
  117.4 7.0 %copy-start.33 = (f32[1,256,256]{2,1,0:T(8,128)S(1)}, f32[1,256,256]{2,1,0:T(8,128)}, u32[]{:S(2)}) copy-start(f32[1,256,256]{2,1,0:T(8,128)} %convolution_bitcast_fusion.7) | copy-start | bytes 786436
  117.4 7.0 %copy-start.34 = (f32[1,256,256]{2,1,0:T(8,128)S(1)}, f32[1,256,256]{2,1,0:T(8,128)}, u32[]{:S(2)}) copy-start(f32[1,256,256]{2,1,0:T(8,128)} %convolution_bitcast_fusion.6) | copy-start | bytes 786436
  130.2 11.6 %collective-permute-start.6 = (f32[266240]{0:T(1024)}, f32[266240]{0:T(1024)}, u32[]{:S(2)}, u32[]{:S(2)}) collective-permute-start(f32[266240]{0:T(1024)} %dynamic_slice.37), channel_id=1, source_target_pairs={{0,1},{1,0},{8,9},{9,8},{16,17},{17,16},{24,25},{25,24},{32,33},{3... | collective-permute-start | bytes 3194888 | tf_op jit(solution)/shard_map/ppermute | solution.py:147
  144.1 13.4 %collective-permute-start.7 = (f32[133120]{0:T(1024)S(1)}, f32[133120]{0:T(1024)S(1)}, u32[]{:S(2)}, u32[]{:S(2)}) collective-permute-start(f32[133120]{0:T(1024)S(1)} %dynamic_slice.39), channel_id=1, source_target_pairs={{0,8},{1,9},{8,0},{9,1},{16,24},{17,25},{24,16},{25,17},{32,40},{3... | collective-permute-start | bytes 1597448 | tf_op jit(solution)/shard_map/ppermute | solution.py:147
  158.6 8.3 %collective-permute-start.8 = (f32[66560]{0:T(1024)S(1)}, f32[66560]{0:T(1024)S(1)}, u32[]{:S(2)}, u32[]{:S(2)}) collective-permute-start(f32[66560]{0:T(1024)S(1)} %dynamic_slice.41), channel_id=1, source_target_pairs={{0,16},{1,17},{8,24},{9,25},{16,0},{17,1},{24,8},{25,9},{32,48},{3... | collective-permute-start | bytes 798728 | tf_op jit(solution)/shard_map/ppermute | solution.py:147
  167.1 3.9 %collective-permute-start.9 = (f32[33280]{0:T(1024)S(1)}, f32[33280]{0:T(1024)S(1)}, u32[]{:S(2)}, u32[]{:S(2)}) collective-permute-start(f32[33280]{0:T(1024)S(1)} %dynamic_slice.43), channel_id=1, source_target_pairs={{0,32},{1,33},{8,40},{9,41},{16,48},{17,49},{24,56},{25,57},{32,0}... | collective-permute-start | bytes 399368 | tf_op jit(solution)/shard_map/ppermute | solution.py:147
  171.3 4.9 %collective-permute-start.10 = (f32[16640]{0:T(1024)S(1)}, f32[16640]{0:T(1024)S(1)}, u32[]{:S(2)}, u32[]{:S(2)}) collective-permute-start(f32[16640]{0:T(1024)S(1)} %dynamic_slice.45), channel_id=1, source_target_pairs={{0,64},{1,65},{8,72},{9,73},{16,80},{17,81},{24,88},{25,89},{32,96... | collective-permute-start | bytes 199688 | tf_op jit(solution)/shard_map/ppermute | solution.py:147
  176.3 7.1 %collective-permute-start.11 = (f32[8320]{0:T(1024)S(1)}, f32[8320]{0:T(1024)S(1)}, u32[]{:S(2)}, u32[]{:S(2)}) collective-permute-start(f32[8320]{0:T(1024)S(1)} %dynamic_slice.47), channel_id=1, source_target_pairs={{0,128},{1,129},{8,136},{9,137},{16,144},{17,145},{24,152},{25,153... | collective-permute-start | bytes 99848 | tf_op jit(solution)/shard_map/ppermute | solution.py:147
  183.5 7.2 %collective-permute-start.12 = (f32[8320]{0:T(1024)S(1)}, f32[8320]{0:T(1024)S(1)}, u32[]{:S(2)}, u32[]{:S(2)}) collective-permute-start(f32[8320]{0:T(1024)S(1)} %dynamic-slice_add_fusion.5), channel_id=1, source_target_pairs={{0,128},{1,129},{8,136},{9,137},{16,144},{17,145},{24,152},{25,153... | collective-permute-start | bytes 99848 | tf_op jit(solution)/shard_map/ppermute | solution.py:151
  190.7 5.0 %collective-permute-start.13 = (f32[16640]{0:T(1024)S(1)}, f32[16640]{0:T(1024)S(1)}, u32[]{:S(2)}, u32[]{:S(2)}) collective-permute-start(f32[16640]{0:T(1024)S(1)} %maximum_select_fusion.9), channel_id=1, source_target_pairs={{0,64},{1,65},{8,72},{9,73},{16,80},{17,81},{24,88},{25,89},{32,96... | collective-permute-start | bytes 199688 | tf_op jit(solution)/shard_map/ppermute | solution.py:151
  195.7 3.9 %collective-permute-start.14 = (f32[33280]{0:T(1024)S(1)}, f32[33280]{0:T(1024)S(1)}, u32[]{:S(2)}, u32[]{:S(2)}) collective-permute-start(f32[33280]{0:T(1024)S(1)} %maximum_select_fusion.8), channel_id=1, source_target_pairs={{0,32},{1,33},{8,40},{9,41},{16,48},{17,49},{24,56},{25,57},{32,0}... | collective-permute-start | bytes 399368 | tf_op jit(solution)/shard_map/ppermute | solution.py:151
  199.7 6.9 %collective-permute-start.15 = (f32[66560]{0:T(1024)S(1)}, f32[66560]{0:T(1024)S(1)}, u32[]{:S(2)}, u32[]{:S(2)}) collective-permute-start(f32[66560]{0:T(1024)S(1)} %maximum_select_fusion.7), channel_id=1, source_target_pairs={{0,16},{1,17},{8,24},{9,25},{16,0},{17,1},{24,8},{25,9},{32,48},{3... | collective-permute-start | bytes 798728 | tf_op jit(solution)/shard_map/ppermute | solution.py:151
  206.6 11.4 %collective-permute-start.16 = (f32[133120]{0:T(1024)S(1)}, f32[133120]{0:T(1024)S(1)}, u32[]{:S(2)}, u32[]{:S(2)}) collective-permute-start(f32[133120]{0:T(1024)S(1)} %maximum_select_fusion.6), channel_id=1, source_target_pairs={{0,8},{1,9},{8,0},{9,1},{16,24},{17,25},{24,16},{25,17},{32,40},{3... | collective-permute-start | bytes 1597448 | tf_op jit(solution)/shard_map/ppermute | solution.py:151
  218.1 10.4 %copy-start.12 = (f32[266240]{0:T(1024)}, f32[266240]{0:T(1024)S(1)}, u32[]{:S(2)}) copy-start(f32[266240]{0:T(1024)S(1)} %maximum_select_fusion.1) | copy-start | bytes 3194884
  218.1 12.8 %collective-permute-start.17 = (f32[266240]{0:T(1024)S(1)}, f32[266240]{0:T(1024)}, u32[]{:S(2)}, u32[]{:S(2)}) collective-permute-start(f32[266240]{0:T(1024)S(1)} %maximum_select_fusion.1), channel_id=1, source_target_pairs={{0,1},{1,0},{8,9},{9,8},{16,17},{17,16},{24,25},{25,24},{32,33},{3... | collective-permute-start | bytes 3194888 | tf_op jit(solution)/shard_map/ppermute | solution.py:151
  (96 other events, 224.4 us)
where the time goes:
time: 242 us; the launch traced here: 241 us
  waiting for transfers between devices  102 us (42%)
  starting transfers between devices  50.8 us (21%)
  matrix products  31.9 us (13%)
  local copies, waits for them, and re-layouts  28 us (12%)
  other arithmetic  24.7 us (10%)
  between operations  3.25 us (1%)
    ppermute x6, waiting for transfers between devices, butterfly_sum(): got = lax.ppermute(send, axes, [(i, i ^ bit) for i in range(count)])  37.6 us
    ppermute x6, waiting for transfers between devices, butterfly_sum(): got = lax.ppermute(buf, axes, [(i, i ^ bit) for i in range(count)])  35.5 us
    dot_general x24, matrix products, outer(): lax.dot_general(first_op, second_op, (((0,), (0,)), ((), ())), preferred_...  19.2 us
    all_to_all x2, waiting for transfers between devices, to_classes(): got = lax.all_to_all(send, 'space', 0, 0, tiled=True)  15.3 us
    all_to_all x2, starting transfers between devices, to_classes(): got = lax.all_to_all(send, 'space', 0, 0, tiled=True)  15.1 us
    ppermute x6, waiting for transfers between devices, recv_from(): return lax.ppermute(block, ('space', 'section'), route)  13.7 us
    ppermute x6, starting transfers between devices, recv_from(): return lax.ppermute(block, ('space', 'section'), route)  12.6 us
    ppermute x6, starting transfers between devices, butterfly_sum(): got = lax.ppermute(send, axes, [(i, i ^ bit) for i in range(count)])  11.6 us
  transfers between devices with their start and end apart: 20, of which 17 were waited for; matrix products, arithmetic and copies ran while one was open for 8% of the time, Pallas kernels for 0%

commit v1 on v0

--- a/solution.py
+++ b/solution.py
@@ -164,6 +164,20 @@
     return jnp.swapaxes(got, 0, 1)[None]
 
 
+def to_classes_both(feats, labels, step, space_count):
+    snaps, rows, cols, channels = feats.shape
+    width = cols // step
+    f = feats.reshape(snaps, rows, width, step, channels).transpose(0, 1, 3, 2, 4)
+    f = f.reshape(space_count, width, channels)
+    l = labels.reshape(snaps, rows, width, step).transpose(0, 1, 3, 2)
+    l = l.reshape(space_count, 1, width).astype(jnp.bfloat16)
+    l = jnp.pad(l, ((0, 0), (0, 0), (0, channels - width)))
+    got = lax.all_to_all(jnp.concatenate([f, l], axis=1), "space", 0, 0, tiled=True)
+    feat_map = jnp.swapaxes(got[:, :width], 0, 1)[None]
+    label_map = jnp.swapaxes(got[:, width, :width], 0, 1)[None].astype(jnp.int32)
+    return feat_map, label_map
+
+
 def per_device(feats, labels, class_weight, depth_kernel, point_weight, proj_weight, head_weight):
     snaps, tile_rows, width_cols, channels = feats.shape
     space_count = lax.axis_size("space")
@@ -177,8 +191,7 @@
     step = tile_rows
     assert snaps * tile_rows * step == space_count and width_cols % step == 0
     assert all(spacing % step == 0 for spacing in spacings)
-    start_map = to_classes(feats, step, space_count)
-    label_map = to_classes(labels, step, space_count)
+    start_map, label_map = to_classes_both(feats, labels, step, space_count)
 
     head_grad = jnp.zeros((channels, 3), jnp.float32)
     saved = None

time: 242 us -> 231 us (0.955)
  waiting for transfers between devices: 102 us -> 94.8 us
  starting transfers between devices: 50.8 us -> 46.5 us
    all_to_all x2 -> x1, waiting for transfers between devices: 15.3 us -> 10.9 us  [to_classes_both(): lax.all_to_all(jnp.concatenate([f, l], axis=1), 'space', 0, 0, tiled=True)]
    all_to_all x2 -> x1, starting transfers between devices: 15.1 us -> 11 us  [to_classes_both(): lax.all_to_all(jnp.concatenate([f, l], axis=1), 'space', 0, 0, tiled=True)]
    unnamed x275 -> x298, local copies, waits for them, and re-layouts: 5.78 us -> 6.72 us
  transfers between devices with their start and end apart: 20 -> 19, of which waited for: 17 -> 16; matrix products, arithmetic and copies ran while one was open for 8% -> 7% of each run, Pallas kernels for 0% -> 0%
where the time goes in v1:
time: 231 us; the launch traced here: 230 us
  waiting for transfers between devices  94.8 us (41%)
  starting transfers between devices  46.5 us (20%)
  matrix products  33.1 us (14%)
  local copies, waits for them, and re-layouts  27 us (12%)
  other arithmetic  24.8 us (11%)
  between operations  3.35 us (1%)
    ppermute x6, waiting for transfers between devices, butterfly_sum(): got = lax.ppermute(send, axes, [(i, i ^ bit) for i in range(count)])  36.1 us
    ppermute x6, waiting for transfers between devices, butterfly_sum(): got = lax.ppermute(buf, axes, [(i, i ^ bit) for i in range(count)])  35.5 us
    dot_general x24, matrix products, outer(): lax.dot_general(first_op, second_op, (((0,), (0,)), ((), ())), preferred_...  19.2 us
    ppermute x6, starting transfers between devices, recv_from(): return lax.ppermute(block, ('space', 'section'), route)  12.6 us
    ppermute x6, waiting for transfers between devices, recv_from(): return lax.ppermute(block, ('space', 'section'), route)  12.3 us
    ppermute x6, starting transfers between devices, butterfly_sum(): got = lax.ppermute(send, axes, [(i, i ^ bit) for i in range(count)])  11.9 us
    all_to_all x1, starting transfers between devices, to_classes_both(): lax.all_to_all(jnp.concatenate([f, l], axis=1), 'space', 0, 0, tiled=True)  11 us
    ppermute x6, starting transfers between devices, butterfly_sum(): got = lax.ppermute(buf, axes, [(i, i ^ bit) for i in range(count)])  10.9 us
  transfers between devices with their start and end apart: 19, of which 16 were waited for; matrix products, arithmetic and copies ran while one was open for 7% of the time, Pallas kernels for 0%

profile of v1, /device:TPU:25, one launch (start us, length us, event | category | flops | bytes accessed | tf_op | source)
XLA Modules:
  0.0 229.6 jit_solution(13636075480661882273)
XLA Ops:
  0.7 1.0 reshape.564
  3.4 11.0 %all-to-all-start = ((bf16[32,11,256]{2,1,0:T(8,128)(2,1)}), bf16[32,11,256]{2,1,0:T(8,128)(2,1)S(1)}, u32[]{:S(2)}, u32[]{:S(2)}) async-start(bf16[32,11,256]{2,1,0:T(8,128)(2,1)} %fusion.466), calls=%async_computation | async-start | bytes 524288 | tf_op jit(solution)/shard_map/all_to_all | solution.py:175
  14.8 10.9 %all-to-all-done = bf16[32,11,256]{2,1,0:T(8,128)(2,1)S(1)} async-done(((bf16[32,11,256]{2,1,0:T(8,128)(2,1)}), bf16[32,11,256]{2,1,0:T(8,128)(2,1)S(1)}, u32[]{:S(2)}, u32[]{:S(2)}) %all-to-all-start) | async-done | bytes 180256 | tf_op jit(solution)/shard_map/all_to_all | solution.py:175
  28.1 1.1 add_convert_fusion.3
  29.2 1.3 collective-permute-start
  32.1 3.2 %collective-permute-done = bf16[1,10,32,256]{3,2,1,0:T(8,128)(2,1)S(1)} collective-permute-done((bf16[1,10,32,256]{3,2,1,0:T(8,128)(2,1)S(1)}, bf16[1,10,32,256]{3,2,1,0:T(8,128)(2,1)S(1)}, u32[]{:S(2)}, u32[]{:S(2)}) %collective-permute-start) | collective-permute-done | bytes 163872 | tf_op jit(solution)/shard_map/ppermute | solution.py:19
  37.4 1.3 collective-permute-start.1
  39.0 4.5 %collective-permute-done.1 = bf16[1,10,32,256]{3,2,1,0:T(8,128)(2,1)S(1)} collective-permute-done((bf16[1,10,32,256]{3,2,1,0:T(8,128)(2,1)S(1)}, bf16[1,10,32,256]{3,2,1,0:T(8,128)(2,1)S(1)}, u32[]{:S(2)}, u32[]{:S(2)}) %collective-permute-start.1) | collective-permute-done | bytes 163872 | tf_op jit(solution)/shard_map/ppermute | solution.py:19
  45.9 1.3 collective-permute-start.2
  47.4 4.6 %collective-permute-done.2 = bf16[1,10,32,256]{3,2,1,0:T(8,128)(2,1)S(1)} collective-permute-done((bf16[1,10,32,256]{3,2,1,0:T(8,128)(2,1)S(1)}, bf16[1,10,32,256]{3,2,1,0:T(8,128)(2,1)S(1)}, u32[]{:S(2)}, u32[]{:S(2)}) %collective-permute-start.2) | collective-permute-done | bytes 163872 | tf_op jit(solution)/shard_map/ppermute | solution.py:19
  52.0 1.1 fusion.611
  59.4 1.6 fusion.7
  61.0 3.0 %collective-permute-start.3 = (bf16[1,10,32,256]{3,2,1,0:T(8,128)(2,1)}, bf16[1,10,32,256]{3,2,1,0:T(8,128)(2,1)}, u32[]{:S(2)}, u32[]{:S(2)}) collective-permute-start(bf16[1,10,32,256]{3,2,1,0:T(8,128)(2,1)} %fusion.7), channel_id=1, source_target_pairs={{2,0},{4,2},{6,4},{10,8},{12,10},{14,12},{18,16},{20,18},{22,20},{... | collective-permute-start | bytes 491528 | tf_op jit(solution)/shard_map/ppermute | solution.py:19
  64.6 1.5 convolution_select_fusion.4
  68.2 1.5 copy.28
  69.7 1.7 reshape.598
  74.5 1.0 convolution_bitcast_fusion.7
  77.8 1.8 collective-permute-start.4
  80.1 1.0 convolution_bitcast_fusion.6
  81.1 1.0 convolution_bitcast_fusion.5
  84.3 1.0 convolution_bitcast_fusion
  85.3 1.0 convolution_bitcast_fusion.4
  86.2 1.0 convolution_bitcast_fusion.11
  87.2 1.0 convolution_bitcast_fusion.10
  90.2 3.9 %collective-permute-start.5 = (bf16[1,10,32,256]{3,2,1,0:T(8,128)(2,1)S(1)}, bf16[1,10,32,256]{3,2,1,0:T(8,128)(2,1)S(1)}, u32[]{:S(2)}, u32[]{:S(2)}) collective-permute-start(bf16[1,10,32,256]{3,2,1,0:T(8,128)(2,1)S(1)} %fusion.354), channel_id=1, source_target_pairs={{2,0},{4,2},{6,4},{10,8},{12,10},{14,12},{18,16},{20,18},{22,20},{... | collective-permute-start | bytes 491528 | tf_op jit(solution)/shard_map/ppermute | solution.py:19
  94.2 1.5 convolution_select_fusion.6
  95.7 1.3 fusion.360
  96.9 1.0 convolution_bitcast_fusion.9
  100.1 1.0 convolution_bitcast_fusion.15
  101.1 1.0 convolution_bitcast_fusion.14
  102.0 1.0 convolution_bitcast_fusion.13
  103.0 1.0 convolution_bitcast_fusion.12
  104.0 1.1 fusion.358
  105.5 1.2 fusion.362
  106.8 1.0 fusion.366
  108.1 1.0 fusion.374
  109.1 1.4 stack.590
  111.3 1.4 stack.556
  112.8 1.3 stack.522
  115.1 2.0 maximum_select_fusion.2
  119.7 1.1 dynamic_slice.37
  120.8 7.6 %collective-permute-start.6 = (f32[266240]{0:T(1024)}, f32[266240]{0:T(1024)}, u32[]{:S(2)}, u32[]{:S(2)}) collective-permute-start(f32[266240]{0:T(1024)} %dynamic_slice.37), channel_id=1, source_target_pairs={{0,1},{1,0},{8,9},{9,8},{16,17},{17,16},{24,25},{25,24},{32,33},{3... | collective-permute-start | bytes 3194888 | tf_op jit(solution)/shard_map/ppermute | solution.py:147
  128.4 2.7 %collective-permute-done.6 = f32[266240]{0:T(1024)} collective-permute-done((f32[266240]{0:T(1024)}, f32[266240]{0:T(1024)}, u32[]{:S(2)}, u32[]{:S(2)}) %collective-permute-start.6) | collective-permute-done | bytes 1064992 | tf_op jit(solution)/shard_map/ppermute | solution.py:147
  131.1 1.3 dynamic-slice_add_fusion
  132.4 1.0 copy-done.13
  133.6 13.2 %collective-permute-done.7 = f32[133120]{0:T(1024)S(1)} collective-permute-done((f32[133120]{0:T(1024)S(1)}, f32[133120]{0:T(1024)S(1)}, u32[]{:S(2)}, u32[]{:S(2)}) %collective-permute-start.7) | collective-permute-done | bytes 532512 | tf_op jit(solution)/shard_map/ppermute | solution.py:147
  146.8 1.1 dynamic-slice_add_fusion.1
  148.0 1.5 collective-permute-start.8
  149.5 6.8 %collective-permute-done.8 = f32[66560]{0:T(1024)S(1)} collective-permute-done((f32[66560]{0:T(1024)S(1)}, f32[66560]{0:T(1024)S(1)}, u32[]{:S(2)}, u32[]{:S(2)}) %collective-permute-start.8) | collective-permute-done | bytes 266272 | tf_op jit(solution)/shard_map/ppermute | solution.py:147
  157.4 3.0 %collective-permute-done.9 = f32[33280]{0:T(1024)S(1)} collective-permute-done((f32[33280]{0:T(1024)S(1)}, f32[33280]{0:T(1024)S(1)}, u32[]{:S(2)}, u32[]{:S(2)}) %collective-permute-start.9) | collective-permute-done | bytes 133152 | tf_op jit(solution)/shard_map/ppermute | solution.py:147
  160.6 1.0 collective-permute-start.10
  161.7 3.8 %collective-permute-done.10 = f32[16640]{0:T(1024)S(1)} collective-permute-done((f32[16640]{0:T(1024)S(1)}, f32[16640]{0:T(1024)S(1)}, u32[]{:S(2)}, u32[]{:S(2)}) %collective-permute-start.10) | collective-permute-done | bytes 66592 | tf_op jit(solution)/shard_map/ppermute | solution.py:147
  166.4 6.5 %collective-permute-done.11 = f32[8320]{0:T(1024)S(1)} collective-permute-done((f32[8320]{0:T(1024)S(1)}, f32[8320]{0:T(1024)S(1)}, u32[]{:S(2)}, u32[]{:S(2)}) %collective-permute-start.11) | collective-permute-done | bytes 33312 | tf_op jit(solution)/shard_map/ppermute | solution.py:147
  173.4 6.5 %collective-permute-done.12 = f32[8320]{0:T(1024)S(1)} collective-permute-done((f32[8320]{0:T(1024)S(1)}, f32[8320]{0:T(1024)S(1)}, u32[]{:S(2)}, u32[]{:S(2)}) %collective-permute-start.12) | collective-permute-done | bytes 33312 | tf_op jit(solution)/shard_map/ppermute | solution.py:151
  180.3 5.0 %collective-permute-done.13 = f32[16640]{0:T(1024)S(1)} collective-permute-done((f32[16640]{0:T(1024)S(1)}, f32[16640]{0:T(1024)S(1)}, u32[]{:S(2)}, u32[]{:S(2)}) %collective-permute-start.13) | collective-permute-done | bytes 66592 | tf_op jit(solution)/shard_map/ppermute | solution.py:151
  185.4 3.8 %collective-permute-done.14 = f32[33280]{0:T(1024)S(1)} collective-permute-done((f32[33280]{0:T(1024)S(1)}, f32[33280]{0:T(1024)S(1)}, u32[]{:S(2)}, u32[]{:S(2)}) %collective-permute-start.14) | collective-permute-done | bytes 133152 | tf_op jit(solution)/shard_map/ppermute | solution.py:151
  189.4 6.8 %collective-permute-done.15 = f32[66560]{0:T(1024)S(1)} collective-permute-done((f32[66560]{0:T(1024)S(1)}, f32[66560]{0:T(1024)S(1)}, u32[]{:S(2)}, u32[]{:S(2)}) %collective-permute-start.15) | collective-permute-done | bytes 266272 | tf_op jit(solution)/shard_map/ppermute | solution.py:151
  196.3 11.0 %collective-permute-done.16 = f32[133120]{0:T(1024)S(1)} collective-permute-done((f32[133120]{0:T(1024)S(1)}, f32[133120]{0:T(1024)S(1)}, u32[]{:S(2)}, u32[]{:S(2)}) %collective-permute-start.16) | collective-permute-done | bytes 532512 | tf_op jit(solution)/shard_map/ppermute | solution.py:151
  207.4 9.9 %collective-permute-start.17 = (f32[266240]{0:T(1024)S(1)}, f32[266240]{0:T(1024)}, u32[]{:S(2)}, u32[]{:S(2)}) collective-permute-start(f32[266240]{0:T(1024)S(1)} %maximum_select_fusion.1), channel_id=1, source_target_pairs={{0,1},{1,0},{8,9},{9,8},{16,17},{17,16},{24,25},{25,24},{32,33},{3... | collective-permute-start | bytes 3194888 | tf_op jit(solution)/shard_map/ppermute | solution.py:151
  217.3 2.4 %collective-permute-done.17 = f32[266240]{0:T(1024)} collective-permute-done((f32[266240]{0:T(1024)S(1)}, f32[266240]{0:T(1024)}, u32[]{:S(2)}, u32[]{:S(2)}) %collective-permute-start.17) | collective-permute-done | bytes 1064992 | tf_op jit(solution)/shard_map/ppermute | solution.py:151
  219.7 2.5 %maximum_select_fusion = f32[532480]{0:T(1024)S(1)} fusion(f32[266240]{0:T(1024)} %copy-done.12, f32[266240]{0:T(1024)} %collective-permute-done.17, pred[]{:T(512)S(6)} %eq.86), kind=kLoop, calls=%fused_computation.4 | loop fusion | flops 1597440 | bytes 4259841 | tf_op jit(solution)/shard_map/jit(_where)/select_n | solution.py:153
  222.2 1.6 fusion.618
  224.2 2.6 %reshape.600 = f32[1,4,256,256]{3,2,1,0:T(8,128)} reshape(f32[262144]{0:T(1024)} %get-tuple-element.227) | data formatting | bytes 2097152 | tf_op jit(solution)/shard_map/reshape | solution.py:238
  226.8 1.3 reshape.601
  (463 shorter events, 41.2 us)
Async XLA Ops:
  0.6 27.5 %copy-start = (bf16[1,1024,256]{2,1,0:T(8,128)(2,1)S(1)}, bf16[1,1024,256]{2,1,0:T(8,128)(2,1)}, u32[]{:S(2)}) copy-start(bf16[1,1024,256]{2,1,0:T(8,128)(2,1)} %param.12) | copy-start | bytes 1572868
  0.6 13.9 %copy-start.106 = (bf16[1,3,9,256]{3,1,2,0:T(4,128)(2,1)S(1)}, bf16[1,3,9,256]{3,1,2,0:T(4,128)(2,1)}, u32[]{:S(2)}) copy-start(bf16[1,3,9,256]{3,1,2,0:T(4,128)(2,1)} %param.10) | copy-start | bytes 41476
  0.7 13.9 %copy-start.146 = (s32[3]{0:T(128)S(1)}, s32[3]{0:T(128)}, u32[]{:S(2)}) copy-start(s32[3]{0:T(128)} %param.9) | copy-start | bytes 40
  3.4 22.3 %all-to-all-start = ((bf16[32,11,256]{2,1,0:T(8,128)(2,1)}), bf16[32,11,256]{2,1,0:T(8,128)(2,1)S(1)}, u32[]{:S(2)}, u32[]{:S(2)}) async-start(bf16[32,11,256]{2,1,0:T(8,128)(2,1)} %fusion.466), calls=%async_computation | async-start | bytes 524288 | tf_op jit(solution)/shard_map/all_to_all | solution.py:175
  14.6 44.1 %copy-start.41 = (f32[1,1,256]{2,0,1:T(1,128)}, f32[1,1,256]{2,0,1:T(1,128)S(1)}, u32[]{:S(2)}) copy-start(f32[1,1,256]{2,0,1:T(1,128)S(1)} %get-tuple-element.302) | copy-start | bytes 3076
  14.6 44.1 %copy-start.43 = (f32[1,1,256]{2,0,1:T(1,128)}, f32[1,1,256]{2,0,1:T(1,128)S(1)}, u32[]{:S(2)}) copy-start(f32[1,1,256]{2,0,1:T(1,128)S(1)} %get-tuple-element.303) | copy-start | bytes 3076
  14.6 44.1 %copy-start.45 = (f32[1,1,256]{2,0,1:T(1,128)}, f32[1,1,256]{2,0,1:T(1,128)S(1)}, u32[]{:S(2)}) copy-start(f32[1,1,256]{2,0,1:T(1,128)S(1)} %get-tuple-element.304) | copy-start | bytes 3076
  14.6 44.1 %copy-start.47 = (f32[1,1,256]{2,0,1:T(1,128)}, f32[1,1,256]{2,0,1:T(1,128)S(1)}, u32[]{:S(2)}) copy-start(f32[1,1,256]{2,0,1:T(1,128)S(1)} %get-tuple-element.305) | copy-start | bytes 3076
  14.6 21.2 %copy-start.78 = (f32[1,1,256]{2,0,1:T(1,128)}, f32[1,1,256]{2,0,1:T(1,128)S(1)}, u32[]{:S(2)}) copy-start(f32[1,1,256]{2,0,1:T(1,128)S(1)} %get-tuple-element.289) | copy-start | bytes 3076
  14.7 21.2 %copy-start.81 = (f32[1,1,256]{2,0,1:T(1,128)}, f32[1,1,256]{2,0,1:T(1,128)S(1)}, u32[]{:S(2)}) copy-start(f32[1,1,256]{2,0,1:T(1,128)S(1)} %get-tuple-element.290) | copy-start | bytes 3076
  14.7 21.2 %copy-start.84 = (f32[1,1,256]{2,0,1:T(1,128)}, f32[1,1,256]{2,0,1:T(1,128)S(1)}, u32[]{:S(2)}) copy-start(f32[1,1,256]{2,0,1:T(1,128)S(1)} %get-tuple-element.291) | copy-start | bytes 3076
  14.7 21.2 %copy-start.87 = (f32[1,1,256]{2,0,1:T(1,128)}, f32[1,1,256]{2,0,1:T(1,128)S(1)}, u32[]{:S(2)}) copy-start(f32[1,1,256]{2,0,1:T(1,128)S(1)} %get-tuple-element.292) | copy-start | bytes 3076
  14.7 21.2 %copy-start.90 = (f32[1,1,256]{2,0,1:T(1,128)}, f32[1,1,256]{2,0,1:T(1,128)S(1)}, u32[]{:S(2)}) copy-start(f32[1,1,256]{2,0,1:T(1,128)S(1)} %get-tuple-element.293) | copy-start | bytes 3076
  14.7 21.2 %copy-start.93 = (f32[1,1,256]{2,0,1:T(1,128)}, f32[1,1,256]{2,0,1:T(1,128)S(1)}, u32[]{:S(2)}) copy-start(f32[1,1,256]{2,0,1:T(1,128)S(1)} %get-tuple-element.294) | copy-start | bytes 3076
  14.7 21.2 %copy-start.96 = (f32[1,1,256]{2,0,1:T(1,128)}, f32[1,1,256]{2,0,1:T(1,128)S(1)}, u32[]{:S(2)}) copy-start(f32[1,1,256]{2,0,1:T(1,128)S(1)} %get-tuple-element.295) | copy-start | bytes 3076
  14.7 21.2 %copy-start.99 = (f32[1,1,256]{2,0,1:T(1,128)}, f32[1,1,256]{2,0,1:T(1,128)S(1)}, u32[]{:S(2)}) copy-start(f32[1,1,256]{2,0,1:T(1,128)S(1)} %get-tuple-element.296) | copy-start | bytes 3076
  14.7 21.2 %copy-start.102 = (f32[1,1,256]{2,0,1:T(1,128)}, f32[1,1,256]{2,0,1:T(1,128)S(1)}, u32[]{:S(2)}) copy-start(f32[1,1,256]{2,0,1:T(1,128)S(1)} %get-tuple-element.297) | copy-start | bytes 3076
  14.7 21.6 %copy-start.51 = (f32[1,1,256]{2,0,1:T(1,128)}, f32[1,1,256]{2,0,1:T(1,128)S(1)}, u32[]{:S(2)}) copy-start(f32[1,1,256]{2,0,1:T(1,128)S(1)} %get-tuple-element.280) | copy-start | bytes 3076
  14.7 21.6 %copy-start.54 = (f32[1,1,256]{2,0,1:T(1,128)}, f32[1,1,256]{2,0,1:T(1,128)S(1)}, u32[]{:S(2)}) copy-start(f32[1,1,256]{2,0,1:T(1,128)S(1)} %get-tuple-element.281) | copy-start | bytes 3076
  14.8 21.6 %copy-start.57 = (f32[1,1,256]{2,0,1:T(1,128)}, f32[1,1,256]{2,0,1:T(1,128)S(1)}, u32[]{:S(2)}) copy-start(f32[1,1,256]{2,0,1:T(1,128)S(1)} %get-tuple-element.282) | copy-start | bytes 3076
  14.8 21.6 %copy-start.60 = (f32[1,1,256]{2,0,1:T(1,128)}, f32[1,1,256]{2,0,1:T(1,128)S(1)}, u32[]{:S(2)}) copy-start(f32[1,1,256]{2,0,1:T(1,128)S(1)} %get-tuple-element.283) | copy-start | bytes 3076
  14.8 21.6 %copy-start.63 = (f32[1,1,256]{2,0,1:T(1,128)}, f32[1,1,256]{2,0,1:T(1,128)S(1)}, u32[]{:S(2)}) copy-start(f32[1,1,256]{2,0,1:T(1,128)S(1)} %get-tuple-element.284) | copy-start | bytes 3076
  14.8 21.6 %copy-start.66 = (f32[1,1,256]{2,0,1:T(1,128)}, f32[1,1,256]{2,0,1:T(1,128)S(1)}, u32[]{:S(2)}) copy-start(f32[1,1,256]{2,0,1:T(1,128)S(1)} %get-tuple-element.285) | copy-start | bytes 3076
  14.8 21.6 %copy-start.69 = (f32[1,1,256]{2,0,1:T(1,128)}, f32[1,1,256]{2,0,1:T(1,128)S(1)}, u32[]{:S(2)}) copy-start(f32[1,1,256]{2,0,1:T(1,128)S(1)} %get-tuple-element.286) | copy-start | bytes 3076
  14.8 21.6 %copy-start.72 = (f32[1,1,256]{2,0,1:T(1,128)}, f32[1,1,256]{2,0,1:T(1,128)S(1)}, u32[]{:S(2)}) copy-start(f32[1,1,256]{2,0,1:T(1,128)S(1)} %get-tuple-element.287) | copy-start | bytes 3076
  14.8 21.6 %copy-start.75 = (f32[1,1,256]{2,0,1:T(1,128)}, f32[1,1,256]{2,0,1:T(1,128)S(1)}, u32[]{:S(2)}) copy-start(f32[1,1,256]{2,0,1:T(1,128)S(1)} %get-tuple-element.288) | copy-start | bytes 3076
  14.8 43.9 %copy-start.49 = (f32[1,1,256]{2,0,1:T(1,128)}, f32[1,1,256]{2,0,1:T(1,128)S(1)}, u32[]{:S(2)}) copy-start(f32[1,1,256]{2,0,1:T(1,128)S(1)} %get-tuple-element.279) | copy-start | bytes 3076
  29.2 6.1 %collective-permute-start = (bf16[1,10,32,256]{3,2,1,0:T(8,128)(2,1)S(1)}, bf16[1,10,32,256]{3,2,1,0:T(8,128)(2,1)S(1)}, u32[]{:S(2)}, u32[]{:S(2)}) collective-permute-start(bf16[1,10,32,256]{3,2,1,0:T(8,128)(2,1)S(1)} %bitcast.584), channel_id=1, source_target_pairs={{0,2},{2,4},{4,6},{8,10},{10,12},{12,14},{16,18},{18,20},{20,22},{... | collective-permute-start | bytes 491528 | tf_op jit(solution)/shard_map/ppermute | solution.py:19
  37.4 6.1 %collective-permute-start.1 = (bf16[1,10,32,256]{3,2,1,0:T(8,128)(2,1)S(1)}, bf16[1,10,32,256]{3,2,1,0:T(8,128)(2,1)S(1)}, u32[]{:S(2)}, u32[]{:S(2)}) collective-permute-start(bf16[1,10,32,256]{3,2,1,0:T(8,128)(2,1)S(1)} %bitcast.585), channel_id=1, source_target_pairs={{0,2},{2,4},{4,6},{8,10},{10,12},{12,14},{16,18},{18,20},{20,22},{... | collective-permute-start | bytes 491528 | tf_op jit(solution)/shard_map/ppermute | solution.py:19
  45.9 6.1 %collective-permute-start.2 = (bf16[1,10,32,256]{3,2,1,0:T(8,128)(2,1)S(1)}, bf16[1,10,32,256]{3,2,1,0:T(8,128)(2,1)S(1)}, u32[]{:S(2)}, u32[]{:S(2)}) collective-permute-start(bf16[1,10,32,256]{3,2,1,0:T(8,128)(2,1)S(1)} %bitcast.586), channel_id=1, source_target_pairs={{0,2},{2,4},{4,6},{8,10},{10,12},{12,14},{16,18},{18,20},{20,22},{... | collective-permute-start | bytes 491528 | tf_op jit(solution)/shard_map/ppermute | solution.py:19
  53.3 10.7 %copy-start.17 = (bf16[1,10,32,256]{3,2,1,0:T(8,128)(2,1)}, bf16[1,10,32,256]{3,2,1,0:T(8,128)(2,1)S(1)}, u32[]{:S(2)}) copy-start(bf16[1,10,32,256]{3,2,1,0:T(8,128)(2,1)S(1)} %get-tuple-element.216) | copy-start | bytes 491524
  53.9 10.4 %copy-start.19 = (bf16[1,10,32,256]{3,2,1,0:T(8,128)(2,1)}, bf16[1,10,32,256]{3,2,1,0:T(8,128)(2,1)S(1)}, u32[]{:S(2)}) copy-start(bf16[1,10,32,256]{3,2,1,0:T(8,128)(2,1)S(1)} %get-tuple-element.218) | copy-start | bytes 491524
  54.4 12.9 %copy-start.21 = (bf16[1,10,32,256]{3,2,1,0:T(8,128)(2,1)}, bf16[1,10,32,256]{3,2,1,0:T(8,128)(2,1)S(1)}, u32[]{:S(2)}) copy-start(bf16[1,10,32,256]{3,2,1,0:T(8,128)(2,1)S(1)} %get-tuple-element.220) | copy-start | bytes 491524
  57.2 7.4 %copy-start.10 = (pred[320,256]{1,0:T(32,128)(4,1)}, pred[320,256]{1,0:T(32,128)(4,1)S(1)}, u32[]{:S(2)}) copy-start(pred[320,256]{1,0:T(32,128)(4,1)S(1)} %select_compare_fusion) | copy-start | bytes 245764
  61.0 11.1 %collective-permute-start.3 = (bf16[1,10,32,256]{3,2,1,0:T(8,128)(2,1)}, bf16[1,10,32,256]{3,2,1,0:T(8,128)(2,1)}, u32[]{:S(2)}, u32[]{:S(2)}) collective-permute-start(bf16[1,10,32,256]{3,2,1,0:T(8,128)(2,1)} %fusion.7), channel_id=1, source_target_pairs={{2,0},{4,2},{6,4},{10,8},{12,10},{14,12},{18,16},{20,18},{22,20},{... | collective-permute-start | bytes 491528 | tf_op jit(solution)/shard_map/ppermute | solution.py:19
  64.6 6.8 %copy-start.28 = (bf16[1,10,32,256]{3,2,1,0:T(8,128)(2,1)S(1)}, bf16[1,10,32,256]{3,2,1,0:T(8,128)(2,1)}, u32[]{:S(2)}) copy-start(bf16[1,10,32,256]{3,2,1,0:T(8,128)(2,1)} %copy-done.27) | copy-start | bytes 491524
  77.8 4.2 %collective-permute-start.4 = (bf16[1,10,32,256]{3,2,1,0:T(8,128)(2,1)S(1)}, bf16[1,10,32,256]{3,2,1,0:T(8,128)(2,1)S(1)}, u32[]{:S(2)}, u32[]{:S(2)}) collective-permute-start(bf16[1,10,32,256]{3,2,1,0:T(8,128)(2,1)S(1)} %fusion.343), channel_id=1, source_target_pairs={{2,0},{4,2},{6,4},{10,8},{12,10},{14,12},{18,16},{20,18},{22,20},{... | collective-permute-start | bytes 491528 | tf_op jit(solution)/shard_map/ppermute | solution.py:19
  90.2 8.6 %collective-permute-start.5 = (bf16[1,10,32,256]{3,2,1,0:T(8,128)(2,1)S(1)}, bf16[1,10,32,256]{3,2,1,0:T(8,128)(2,1)S(1)}, u32[]{:S(2)}, u32[]{:S(2)}) collective-permute-start(bf16[1,10,32,256]{3,2,1,0:T(8,128)(2,1)S(1)} %fusion.354), channel_id=1, source_target_pairs={{2,0},{4,2},{6,4},{10,8},{12,10},{14,12},{18,16},{20,18},{22,20},{... | collective-permute-start | bytes 491528 | tf_op jit(solution)/shard_map/ppermute | solution.py:19
  107.9 6.3 %copy-start.127 = (f32[256]{0:T(256)S(1)}, f32[256]{0:T(256)}, u32[]{:S(2)}) copy-start(f32[256]{0:T(256)} %get-tuple-element.181) | copy-start | bytes 3076
  107.9 6.3 %copy-start.128 = (f32[256]{0:T(256)S(1)}, f32[256]{0:T(256)}, u32[]{:S(2)}) copy-start(f32[256]{0:T(256)} %get-tuple-element.182) | copy-start | bytes 3076
  107.9 6.3 %copy-start.129 = (f32[256]{0:T(256)S(1)}, f32[256]{0:T(256)}, u32[]{:S(2)}) copy-start(f32[256]{0:T(256)} %get-tuple-element.183) | copy-start | bytes 3076
  108.0 6.3 %copy-start.123 = (f32[256]{0:T(256)S(1)}, f32[256]{0:T(256)}, u32[]{:S(2)}) copy-start(f32[256]{0:T(256)} %get-tuple-element.184) | copy-start | bytes 3076
  108.0 6.3 %copy-start.124 = (f32[256]{0:T(256)S(1)}, f32[256]{0:T(256)}, u32[]{:S(2)}) copy-start(f32[256]{0:T(256)} %get-tuple-element.185) | copy-start | bytes 3076
  108.0 6.3 %copy-start.125 = (f32[256]{0:T(256)S(1)}, f32[256]{0:T(256)}, u32[]{:S(2)}) copy-start(f32[256]{0:T(256)} %get-tuple-element.188) | copy-start | bytes 3076
  108.0 6.3 %copy-start.126 = (f32[256]{0:T(256)S(1)}, f32[256]{0:T(256)}, u32[]{:S(2)}) copy-start(f32[256]{0:T(256)} %get-tuple-element.189) | copy-start | bytes 3076
  108.0 6.3 %copy-start.142 = (f32[256]{0:T(256)S(1)}, f32[256]{0:T(256)}, u32[]{:S(2)}) copy-start(f32[256]{0:T(256)} %get-tuple-element.134) | copy-start | bytes 3076
  108.0 6.3 %copy-start.143 = (f32[256]{0:T(256)S(1)}, f32[256]{0:T(256)}, u32[]{:S(2)}) copy-start(f32[256]{0:T(256)} %get-tuple-element.135) | copy-start | bytes 3076
  108.0 6.3 %copy-start.144 = (f32[256]{0:T(256)S(1)}, f32[256]{0:T(256)}, u32[]{:S(2)}) copy-start(f32[256]{0:T(256)} %get-tuple-element.166) | copy-start | bytes 3076
  108.0 7.0 %copy-start.32 = (f32[1,256,256]{2,1,0:T(8,128)S(1)}, f32[1,256,256]{2,1,0:T(8,128)}, u32[]{:S(2)}) copy-start(f32[1,256,256]{2,1,0:T(8,128)} %convolution_bitcast_fusion.1) | copy-start | bytes 786436
  108.1 7.0 %copy-start.33 = (f32[1,256,256]{2,1,0:T(8,128)S(1)}, f32[1,256,256]{2,1,0:T(8,128)}, u32[]{:S(2)}) copy-start(f32[1,256,256]{2,1,0:T(8,128)} %convolution_bitcast_fusion.7) | copy-start | bytes 786436
  108.1 7.0 %copy-start.34 = (f32[1,256,256]{2,1,0:T(8,128)S(1)}, f32[1,256,256]{2,1,0:T(8,128)}, u32[]{:S(2)}) copy-start(f32[1,256,256]{2,1,0:T(8,128)} %convolution_bitcast_fusion.6) | copy-start | bytes 786436
  120.8 10.3 %collective-permute-start.6 = (f32[266240]{0:T(1024)}, f32[266240]{0:T(1024)}, u32[]{:S(2)}, u32[]{:S(2)}) collective-permute-start(f32[266240]{0:T(1024)} %dynamic_slice.37), channel_id=1, source_target_pairs={{0,1},{1,0},{8,9},{9,8},{16,17},{17,16},{24,25},{25,24},{32,33},{3... | collective-permute-start | bytes 3194888 | tf_op jit(solution)/shard_map/ppermute | solution.py:147
  133.5 13.4 %collective-permute-start.7 = (f32[133120]{0:T(1024)S(1)}, f32[133120]{0:T(1024)S(1)}, u32[]{:S(2)}, u32[]{:S(2)}) collective-permute-start(f32[133120]{0:T(1024)S(1)} %dynamic_slice.39), channel_id=1, source_target_pairs={{0,8},{1,9},{8,0},{9,1},{16,24},{17,25},{24,16},{25,17},{32,40},{3... | collective-permute-start | bytes 1597448 | tf_op jit(solution)/shard_map/ppermute | solution.py:147
  148.0 8.3 %collective-permute-start.8 = (f32[66560]{0:T(1024)S(1)}, f32[66560]{0:T(1024)S(1)}, u32[]{:S(2)}, u32[]{:S(2)}) collective-permute-start(f32[66560]{0:T(1024)S(1)} %dynamic_slice.41), channel_id=1, source_target_pairs={{0,16},{1,17},{8,24},{9,25},{16,0},{17,1},{24,8},{25,9},{32,48},{3... | collective-permute-start | bytes 798728 | tf_op jit(solution)/shard_map/ppermute | solution.py:147
  156.4 3.9 %collective-permute-start.9 = (f32[33280]{0:T(1024)S(1)}, f32[33280]{0:T(1024)S(1)}, u32[]{:S(2)}, u32[]{:S(2)}) collective-permute-start(f32[33280]{0:T(1024)S(1)} %dynamic_slice.43), channel_id=1, source_target_pairs={{0,32},{1,33},{8,40},{9,41},{16,48},{17,49},{24,56},{25,57},{32,0}... | collective-permute-start | bytes 399368 | tf_op jit(solution)/shard_map/ppermute | solution.py:147
  160.6 4.9 %collective-permute-start.10 = (f32[16640]{0:T(1024)S(1)}, f32[16640]{0:T(1024)S(1)}, u32[]{:S(2)}, u32[]{:S(2)}) collective-permute-start(f32[16640]{0:T(1024)S(1)} %dynamic_slice.45), channel_id=1, source_target_pairs={{0,64},{1,65},{8,72},{9,73},{16,80},{17,81},{24,88},{25,89},{32,96... | collective-permute-start | bytes 199688 | tf_op jit(solution)/shard_map/ppermute | solution.py:147
  165.7 7.3 %collective-permute-start.11 = (f32[8320]{0:T(1024)S(1)}, f32[8320]{0:T(1024)S(1)}, u32[]{:S(2)}, u32[]{:S(2)}) collective-permute-start(f32[8320]{0:T(1024)S(1)} %dynamic_slice.47), channel_id=1, source_target_pairs={{0,128},{1,129},{8,136},{9,137},{16,144},{17,145},{24,152},{25,153... | collective-permute-start | bytes 99848 | tf_op jit(solution)/shard_map/ppermute | solution.py:147
  173.0 6.8 %collective-permute-start.12 = (f32[8320]{0:T(1024)S(1)}, f32[8320]{0:T(1024)S(1)}, u32[]{:S(2)}, u32[]{:S(2)}) collective-permute-start(f32[8320]{0:T(1024)S(1)} %dynamic-slice_add_fusion.5), channel_id=1, source_target_pairs={{0,128},{1,129},{8,136},{9,137},{16,144},{17,145},{24,152},{25,153... | collective-permute-start | bytes 99848 | tf_op jit(solution)/shard_map/ppermute | solution.py:151
  179.9 5.4 %collective-permute-start.13 = (f32[16640]{0:T(1024)S(1)}, f32[16640]{0:T(1024)S(1)}, u32[]{:S(2)}, u32[]{:S(2)}) collective-permute-start(f32[16640]{0:T(1024)S(1)} %maximum_select_fusion.9), channel_id=1, source_target_pairs={{0,64},{1,65},{8,72},{9,73},{16,80},{17,81},{24,88},{25,89},{32,96... | collective-permute-start | bytes 199688 | tf_op jit(solution)/shard_map/ppermute | solution.py:151
  185.3 3.9 %collective-permute-start.14 = (f32[33280]{0:T(1024)S(1)}, f32[33280]{0:T(1024)S(1)}, u32[]{:S(2)}, u32[]{:S(2)}) collective-permute-start(f32[33280]{0:T(1024)S(1)} %maximum_select_fusion.8), channel_id=1, source_target_pairs={{0,32},{1,33},{8,40},{9,41},{16,48},{17,49},{24,56},{25,57},{32,0}... | collective-permute-start | bytes 399368 | tf_op jit(solution)/shard_map/ppermute | solution.py:151
  189.3 6.9 %collective-permute-start.15 = (f32[66560]{0:T(1024)S(1)}, f32[66560]{0:T(1024)S(1)}, u32[]{:S(2)}, u32[]{:S(2)}) collective-permute-start(f32[66560]{0:T(1024)S(1)} %maximum_select_fusion.7), channel_id=1, source_target_pairs={{0,16},{1,17},{8,24},{9,25},{16,0},{17,1},{24,8},{25,9},{32,48},{3... | collective-permute-start | bytes 798728 | tf_op jit(solution)/shard_map/ppermute | solution.py:151
  196.2 11.1 %collective-permute-start.16 = (f32[133120]{0:T(1024)S(1)}, f32[133120]{0:T(1024)S(1)}, u32[]{:S(2)}, u32[]{:S(2)}) collective-permute-start(f32[133120]{0:T(1024)S(1)} %maximum_select_fusion.6), channel_id=1, source_target_pairs={{0,8},{1,9},{8,0},{9,1},{16,24},{17,25},{24,16},{25,17},{32,40},{3... | collective-permute-start | bytes 1597448 | tf_op jit(solution)/shard_map/ppermute | solution.py:151
  207.4 9.9 %copy-start.12 = (f32[266240]{0:T(1024)}, f32[266240]{0:T(1024)S(1)}, u32[]{:S(2)}) copy-start(f32[266240]{0:T(1024)S(1)} %maximum_select_fusion.1) | copy-start | bytes 3194884
  207.4 12.3 %collective-permute-start.17 = (f32[266240]{0:T(1024)S(1)}, f32[266240]{0:T(1024)}, u32[]{:S(2)}, u32[]{:S(2)}) collective-permute-start(f32[266240]{0:T(1024)S(1)} %maximum_select_fusion.1), channel_id=1, source_target_pairs={{0,1},{1,0},{8,9},{9,8},{16,17},{17,16},{24,25},{25,24},{32,33},{3... | collective-permute-start | bytes 3194888 | tf_op jit(solution)/shard_map/ppermute | solution.py:151
  (106 other events, 243.6 us)
